TPU v7x, 256 devices: a whole 4x4x8 slice. The times are simulated.
256 devices in a mesh: seq: 32 (over x, z), mp: 8 (over y, core).
Axes of the slice: x: 4, y: 4, z: 8, core: 2. Of those that a mesh axis runs over, the one named last changes fastest.
Arguments:
- frames: bfloat16 [36864, 1024], P('seq', 'mp'), may hold values from -6 to 6
- keep_flags: int32 [36864], P('seq'), may hold values from 0 to 1, as said below
- pack_rows: int32 [12288], P('seq'), may hold values from 0 to 12287, as said below
- ln_gains: float32 [2, 1024], replicated, may hold values from 0.25 to 1.75
- w_qkv: bfloat16 [1024, 3, 1024], P(None, None, 'mp'), may hold values from -0.1875 to 0.1875, as said below
- w_attn_out: bfloat16 [1024, 1024], P('mp'), may hold values from -0.5 to 0.5
- w_up: bfloat16 [1024, 4096], P(None, 'mp'), may hold values from -0.1875 to 0.1875
- w_down: bfloat16 [4096, 1024], P('mp'), may hold values from -0.09375 to 0.09375
- mask_emb: bfloat16 [1024], replicated, may hold values from -5 to 5
- w_dec_in: bfloat16 [1024, 768], P(None, 'mp'), may hold values from -0.1875 to 0.1875
- w_conv: bfloat16 [4, 7, 768, 48], P(None, None, 'mp'), may hold values from -0.3125 to 0.3125
- w_dec_out: bfloat16 [768, 1024], P('mp'), may hold values from -0.21875 to 0.21875
- targets: bfloat16 [1024, 36864], P('mp', 'seq'), may hold values from -6 to 6
Outputs:
- student_rows: bfloat16 [12288, 1024], P('seq', 'mp')
- pred_error: bfloat16 [1024, 36864], P('mp', 'seq')
Inputs may be any that keep to these rules, and one draw needn't show every extreme that they name: `keep_flags`: in each aligned group of four blocks of 1152 frames exactly 1536 frames are kept, and no block keeps more than 768; in some group the first block keeps exactly 768. In all 12288 frames are kept. `pack_rows`: each aligned block of 384 entries is a permutation of the same block of packed rows. `w_qkv`: entries are of the size of a projection with 1024 inputs.
All inputs are finite; a program needn't handle non-finite values.
Results may differ from a plain program's by a relative error of at most 0.019.
Values may be sent and summed in bfloat16 or wider, within the bound.
No kernel may reach another device: no remote copies, remote signals or barrier semaphores. Data moves between devices by JAX's collectives and lax.ppermute only.
A program may use at most 64 MiB of HBM per device.

v0:
```python
import math

import jax
import jax.numpy as jnp
from jax import lax
from jax.sharding import PartitionSpec as P

HEAD_DIM = 64
C = 768
CG = 48
KW = 7
BLOCKS = 4


NORM_EPSILON = 1e-05


def with_halo(block, sides, width):
    for axis, dim in sides:
        count = lax.axis_size(axis)
        forward = [(i, i + 1) for i in range(count - 1)]
        backward = [(target, source) for source, target in forward]
        low = lax.ppermute(
            lax.slice_in_dim(block, block.shape[dim] - width, None, axis=dim), axis, forward
        )
        high = lax.ppermute(lax.slice_in_dim(block, 0, width, axis=dim), axis, backward)
        block = jnp.concatenate([low, block, high], axis=dim)
    return block


def gather_all(values, axis):
    count = lax.axis_size(axis)
    spread = jnp.broadcast_to(values[None], (count,) + values.shape)
    return lax.all_to_all(spread, axis, 0, 0, tiled=True)


def sum_scatter(pieces, axis, dim):
    count = lax.axis_size(axis)
    shape = pieces.shape
    split = pieces.reshape(shape[:dim] + (count, shape[dim] // count) + shape[dim + 1 :])
    moved = lax.all_to_all(split, axis, dim, dim, tiled=True)
    return jnp.sum(moved.astype(jnp.float32), axis=dim)


def layer_norm(values, gain):
    values = values.astype(jnp.float32)
    centre = jnp.mean(values, axis=-1, keepdims=True)
    spread = jnp.mean(jnp.square(values - centre), axis=-1, keepdims=True)
    return (values - centre) * lax.rsqrt(spread + NORM_EPSILON) * gain


def rounded(values):
    return lax.optimization_barrier(values.astype(jnp.bfloat16)).astype(jnp.float32)


def local(
    frames,
    keep_flags,
    pack_rows,
    ln_gains,
    w_qkv,
    w_attn_out,
    w_up,
    w_down,
    mask_emb,
    w_dec_in,
    w_conv,
    w_dec_out,
    targets,
):
    frame_count = keep_flags.shape[0]
    slot_rows = pack_rows.shape[0]
    feature_width = frames.shape[1]
    seq_devices = lax.axis_size("seq")
    seq_index = lax.axis_index("seq")
    capacity = (2 * slot_rows + seq_devices - 1) // seq_devices
    kept_count = jnp.sum(keep_flags)
    counts_all = gather_all(kept_count[None], "seq").reshape(seq_devices)
    starts_all = jnp.cumsum(counts_all) - counts_all
    kept_before = starts_all[seq_index]
    local_rank = jnp.cumsum(keep_flags) - keep_flags
    frame_index = jnp.arange(frame_count, dtype=jnp.int32)
    kept_where = (
        jnp.zeros((frame_count,), jnp.int32)
        .at[jnp.where(keep_flags == 1, local_rank, frame_count)]
        .set(frame_index, mode="drop")
    )
    slot_steps = jnp.arange(capacity, dtype=jnp.int32)[None, :] * seq_devices
    owners = jnp.arange(seq_devices, dtype=jnp.int32)
    first_sent = kept_before + (owners - kept_before) % seq_devices
    offset = first_sent[:, None] + slot_steps - kept_before
    inside = offset < kept_count
    source = kept_where[jnp.clip(offset, 0, frame_count - 1)]
    outgoing = jnp.where(inside[..., None], frames[source], jnp.zeros((), jnp.bfloat16))
    incoming = lax.all_to_all(outgoing, "seq", split_axis=0, concat_axis=0, tiled=True)
    first_got = starts_all + (seq_index - starts_all) % seq_devices
    ranks_got = first_got[:, None] + slot_steps
    valid = ranks_got < (starts_all + counts_all)[:, None]
    places = jnp.where(valid, ranks_got // seq_devices, slot_rows).reshape(-1)
    by_rank = (
        jnp.zeros((slot_rows, feature_width), jnp.bfloat16)
        .at[places]
        .set(incoming.reshape(-1, feature_width), mode="drop")
    )
    local_row = pack_rows - seq_index * slot_rows
    inverse = (
        jnp.zeros((slot_rows,), jnp.int32).at[local_row].set(jnp.arange(slot_rows, dtype=jnp.int32))
    )
    packed = by_rank[inverse]
    heads_local = feature_width // HEAD_DIM
    gathered = lax.all_gather(packed, "mp", axis=1, tiled=True)
    normed = layer_norm(gathered, ln_gains[0]).astype(jnp.bfloat16)
    projected = jnp.dot(
        normed, w_qkv.reshape(w_qkv.shape[0], -1), preferred_element_type=jnp.float32
    ).astype(jnp.bfloat16)
    queries = projected[:, :feature_width].reshape(slot_rows, heads_local, HEAD_DIM)
    score_scale = 1.0 / math.sqrt(HEAD_DIM)
    start_state = (
        jnp.full((heads_local, slot_rows), -jnp.inf, jnp.float32),
        jnp.zeros((heads_local, slot_rows), jnp.float32),
        jnp.zeros((slot_rows, heads_local, HEAD_DIM), jnp.float32),
    )
    carry = start_state
    key_value = lax.all_gather(projected[:, feature_width:], "seq", axis=0, tiled=True)
    piece_keys = key_value[:, :feature_width]
    piece_values = key_value[:, feature_width:]
    piece_rows = piece_keys.shape[0]
    block_rows = math.gcd(piece_rows, 512)
    piece_keys = piece_keys.reshape(piece_rows // block_rows, block_rows, heads_local, HEAD_DIM)
    piece_values = piece_values.reshape(piece_rows // block_rows, block_rows, heads_local, HEAD_DIM)

    def advance(state, block_pair):
        running_max, totals, weighted = state
        block_keys, block_values = block_pair
        scores = (
            jnp.einsum("qhd,khd->hqk", queries, block_keys, preferred_element_type=jnp.float32)
            * score_scale
        )
        new_max = jnp.maximum(running_max, jnp.max(scores, axis=2))
        factor = jnp.exp(running_max - new_max)
        expo = jnp.exp(scores - new_max[:, :, None])
        totals = totals * factor + jnp.sum(expo, axis=2)
        weighted = weighted * jnp.transpose(factor)[:, :, None] + jnp.einsum(
            "hqk,khd->qhd",
            expo.astype(jnp.bfloat16),
            block_values,
            preferred_element_type=jnp.float32,
        )
        return ((new_max, totals, weighted), None)

    carry, _ = lax.scan(advance, carry, (piece_keys, piece_values))
    running_max, totals, weighted = carry
    attended = (
        (weighted / jnp.transpose(totals)[:, :, None])
        .reshape(slot_rows, feature_width)
        .astype(jnp.bfloat16)
    )
    attn_terms = rounded(jnp.dot(attended, w_attn_out, preferred_element_type=jnp.float32))
    attn_mixed = sum_scatter(attn_terms.astype(jnp.bfloat16), "mp", 1)
    first_out = (packed.astype(jnp.float32) + attn_mixed).astype(jnp.bfloat16)
    gathered_two = lax.all_gather(first_out, "mp", axis=1, tiled=True)
    normed_two = layer_norm(gathered_two, ln_gains[1]).astype(jnp.bfloat16)
    hidden = jax.nn.gelu(
        jnp.dot(normed_two, w_up, preferred_element_type=jnp.float32), approximate=False
    ).astype(jnp.bfloat16)
    mlp_terms = rounded(jnp.dot(hidden, w_down, preferred_element_type=jnp.float32))
    mlp_mixed = sum_scatter(mlp_terms.astype(jnp.bfloat16), "mp", 1)
    student_rows = (first_out.astype(jnp.float32) + mlp_mixed).astype(jnp.bfloat16)
    filler = lax.dynamic_slice_in_dim(
        mask_emb, lax.axis_index("mp") * feature_width, feature_width, 0
    )
    by_rank_out = student_rows[local_row]
    back_out = by_rank_out[jnp.clip(places, 0, slot_rows - 1)].reshape(
        seq_devices, capacity, feature_width
    )
    back_in = lax.all_to_all(back_out, "seq", 0, 0, tiled=True).reshape(-1, feature_width)
    back_index = ((kept_before + local_rank) % seq_devices) * capacity + local_rank // seq_devices
    returned = back_in[jnp.clip(back_index, 0, seq_devices * capacity - 1)]
    grid_rows = jnp.where(keep_flags[:, None] == 1, returned, filler[None, :])
    mp_devices = lax.axis_size("mp")
    mp_index = lax.axis_index("mp")
    span = frame_count // mp_devices
    halo = (KW // 2) * BLOCKS
    own_frames = lax.all_to_all(
        grid_rows.reshape(mp_devices, span, feature_width), "mp", 0, 2, tiled=True
    ).reshape(span, mp_devices * feature_width)
    dec_in_full = lax.all_gather(w_dec_in, "mp", axis=1, tiled=True)
    conv_full = lax.all_gather(
        w_conv.reshape(w_conv.shape[:2] + (-1, CG, CG)), "mp", axis=2, tiled=True
    )
    dec_out_full = lax.all_gather(w_dec_out, "mp", axis=0, tiled=True)
    activity = lax.dot_general(
        dec_in_full, own_frames, (((0,), (1,)), ((), ())), preferred_element_type=jnp.float32
    ).astype(jnp.bfloat16)
    both = ("seq", "mp")
    place = seq_index * mp_devices + mp_index
    places_total = seq_devices * mp_devices
    forward = [(i, i + 1) for i in range(places_total - 1)]
    backward = [(i + 1, i) for i in range(places_total - 1)]
    low = lax.ppermute(activity[:, span - halo :], both, forward)
    high = lax.ppermute(activity[:, :halo], both, backward)
    activity = jnp.concatenate([low, activity, high], axis=1)
    frame_at = place * span - halo + jnp.arange(span + 2 * halo, dtype=jnp.int32)
    in_range = (frame_at >= 0) & (frame_at < places_total * span)
    groups = C // CG
    for block_id in range(BLOCKS):
        width = activity.shape[1] - (KW - 1)
        kernel = conv_full[block_id]
        conv = jnp.zeros((groups, CG, width), jnp.float32)
        for tap_index in range(KW):
            tap = activity[:, tap_index : tap_index + width].reshape(groups, CG, width)
            conv = conv + jnp.einsum(
                "goi,gif->gof", kernel[tap_index], tap, preferred_element_type=jnp.float32
            )
        conv = conv.reshape(C, width)
        centre = jnp.mean(conv, axis=0)
        square_mean = jnp.mean(conv * conv, axis=0)
        normal = (conv - centre) * lax.rsqrt(square_mean - centre * centre + NORM_EPSILON)
        result = jax.nn.gelu(normal, approximate=False)
        if block_id > 0:
            result = result + activity[:, KW // 2 : KW // 2 + width].astype(jnp.float32)
        lower = (block_id + 1) * (KW // 2)
        result = jnp.where(in_range[lower : lower + width][None, :], result, 0.0)
        activity = result.astype(jnp.bfloat16)
    part_height = C // mp_devices
    pieces = jnp.einsum(
        "jcd,jcf->jdf",
        dec_out_full.reshape(mp_devices, part_height, -1),
        activity.reshape(mp_devices, part_height, span),
        preferred_element_type=jnp.float32,
    )
    predicted = jnp.sum(rounded(pieces), axis=0)
    own_targets = lax.all_to_all(
        targets.reshape(targets.shape[0], mp_devices, span), "mp", 1, 0, tiled=True
    ).reshape(-1, span)
    own_keep = lax.dynamic_slice_in_dim(keep_flags, mp_index * span, span, 0)
    masked = (1 - own_keep).astype(jnp.float32)[None, :]
    own_error = ((predicted - own_targets.astype(jnp.float32)) * masked).astype(jnp.bfloat16)
    pred_error = lax.all_to_all(
        own_error.reshape(mp_devices, -1, span), "mp", 0, 2, tiled=True
    ).reshape(-1, frame_count)
    return (student_rows, pred_error)


def solution(mesh):
    return jax.shard_map(
        local,
        mesh=mesh,
        in_specs=(
            P("seq", "mp"),
            P("seq"),
            P("seq"),
            P(),
            P(None, None, "mp"),
            P("mp", None),
            P(None, "mp"),
            P("mp", None),
            P(),
            P(None, "mp"),
            P(None, None, "mp", None),
            P("mp", None),
            P("mp", "seq"),
        ),
        out_specs=(P("seq", "mp"), P("mp", "seq")),
        check_vma=False,
    )
```

profile of v0, /device:TPU:1, one launch (start us, length us, event | category | flops | bytes accessed | tf_op | source)
XLA Modules:
  0.0 449.8 jit_solution(13335605557011199212)
XLA Ops:
  7.2 1.4 reduce_sum.155
  9.9 11.9 %all-to-all-start = ((s32[32,1,1]{2,1,0:T(1,128)}), s32[32,1,1]{2,1,0:T(1,128)S(1)}, u32[]{:S(2)}, u32[]{:S(2)}) async-start(s32[32,1,1]{2,1,0:T(1,128)} %broadcast_in_dim.95), calls=%async_computation | async-start | bytes 32768 | tf_op jit(solution)/shard_map/all_to_all | solution.py:34
  23.6 2.9 scatter_custom_fusion.2
  27.3 3.0 all-to-all-done
  33.1 1.4 subtract_compare_fusion
  34.6 1.4 compare_select_fusion.2
  36.1 6.4 %scatter_custom_fusion = s32[1152]{0:T(1024)S(1)} fusion(s32[1152]{0:T(1024)S(1)} %get-tuple-element.164, s32[1152]{0:T(1024)S(1)} %iota.25, s32[]{:T(128)} %constant.70.clone.1), kind=kCustom, calls=%fused_computation.316 | custom fusion | bytes 4612 | tf_op jit(solution)/shard_map/scatter | solution.py:86
  42.5 4.5 gather_fusion
  47.2 1.9 gather_fusion.1
  49.9 6.3 %all-to-all-start.1 = ((bf16[32,24,128]{2,1,0:T(8,128)(2,1)}), bf16[32,24,128]{2,1,0:T(8,128)(2,1)S(1)}, u32[]{:S(2)}, u32[]{:S(2)}) async-start(bf16[32,24,128]{2,1,0:T(8,128)(2,1)} %broadcast_select_fusion.2), calls=%async_computation.1 | async-start | bytes 393216 | tf_op jit(solution)/shard_map/all_to_all | solution.py:95
  57.8 7.8 %all-to-all-done.1 = bf16[32,24,128]{2,1,0:T(8,128)(2,1)S(1)} async-done(((bf16[32,24,128]{2,1,0:T(8,128)(2,1)}), bf16[32,24,128]{2,1,0:T(8,128)(2,1)S(1)}, u32[]{:S(2)}, u32[]{:S(2)}) %all-to-all-start.1) | async-done | bytes 196640 | tf_op jit(solution)/shard_map/all_to_all | solution.py:95
  65.6 4.2 scatter_custom_fusion.1
  69.9 1.4 gather_fusion.2
  71.3 17.1 %all-gather = bf16[384,1024]{1,0:T(8,128)(2,1)S(1)} all-gather(bf16[384,128]{1,0:T(8,128)(2,1)S(1)} %gather_fusion.2), channel_id=2, replica_groups=mesh['seq'=32,'mp'=8] {'mp'}, dimensions={1}, use_global_device_ids=true | all-gather | bytes 884736 | tf_op jit(solution)/shard_map/all_gather | solution.py:111
  91.3 82.1 %all-gather.6.cloned.1.call-done = bf16[12288,256]{0,1:T(8,128)(2,1)} async-done(((bf16[384,256]{0,1:T(8,128)(2,1)}), bf16[12288,256]{0,1:T(8,128)(2,1)}) %all-gather.6.cloned.1.call-update) | async-done | bytes 6291472 | tf_op jit(solution)/shard_map/all_gather | solution.py:124
  173.4 3.2 fusion.189
  177.9 2.7 copy.165
  181.9 2.7 copy.166
  184.6 70.5 %while.15 = (s32[]{:T(128)}, f32[2,384]{1,0:T(2,128)S(1)}, f32[2,384]{1,0:T(2,128)S(1)}, f32[384,2,64]{0,2,1:T(8,128)S(1)}, bf16[24,512,2,64]{1,3,2,0:T(8,128)(2...) while((s32[]{:T(128)}, f32[2,384]{1,0:T(2,128)S(1)}, ...), condition=%wide.region_12.13_spmd.clone, body=%wide.region_9.12_spmd.clone.sunk | while | flops 103174656 | bytes 5522537 | solution.py:151
  184.6 1.4 bitcast_reduce_fusion.2
  187.6 1.3 bitcast_reduce_fusion.2
  190.6 1.3 bitcast_reduce_fusion.2
  191.9 1.3 fusion.251
  193.5 1.3 bitcast_reduce_fusion.2
  196.5 1.3 bitcast_reduce_fusion.2
  199.4 1.3 bitcast_reduce_fusion.2
  202.4 1.3 bitcast_reduce_fusion.2
  205.3 1.3 bitcast_reduce_fusion.2
  208.2 1.3 bitcast_reduce_fusion.2
  211.2 1.3 bitcast_reduce_fusion.2
  214.1 1.3 bitcast_reduce_fusion.2
  217.0 1.3 bitcast_reduce_fusion.2
  220.0 1.3 bitcast_reduce_fusion.2
  222.9 1.3 bitcast_reduce_fusion.2
  225.8 1.3 bitcast_reduce_fusion.2
  228.8 1.3 bitcast_reduce_fusion.2
  231.7 1.3 bitcast_reduce_fusion.2
  234.7 1.3 bitcast_reduce_fusion.2
  237.6 1.3 bitcast_reduce_fusion.2
  240.5 1.3 bitcast_reduce_fusion.2
  243.5 1.3 bitcast_reduce_fusion.2
  246.4 1.3 bitcast_reduce_fusion.2
  249.3 1.3 bitcast_reduce_fusion.2
  252.3 1.3 bitcast_reduce_fusion.2
  256.7 7.5 %all-to-all-start.2 = ((bf16[384,8,128]{2,0,1:T(8,128)(2,1)}), bf16[384,8,128]{2,0,1:T(8,128)(2,1)S(1)}, u32[]{:S(2)}, u32[]{:S(2)}) async-start(bf16[384,8,128]{2,0,1:T(8,128)(2,1)} %copy_bitcast_fusion.1), calls=%async_computation.2 | async-start | bytes 1572864 | tf_op jit(solution)/shard_map/all_to_all | solution.py:41
  265.4 11.0 %all-to-all-done.2 = bf16[384,8,128]{2,0,1:T(8,128)(2,1)S(1)} async-done(((bf16[384,8,128]{2,0,1:T(8,128)(2,1)}), bf16[384,8,128]{2,0,1:T(8,128)(2,1)S(1)}, u32[]{:S(2)}, u32[]{:S(2)}) %all-to-all-start.2) | async-done | bytes 786464 | tf_op jit(solution)/shard_map/all_to_all | solution.py:41
  276.5 16.4 %all_gather.20 = bf16[384,1024]{1,0:T(8,128)(2,1)S(1)} all-gather(bf16[384,128]{1,0:T(8,128)(2,1)S(1)} %add_convert_fusion.1), channel_id=1, replica_groups=mesh['seq'=32,'mp'=8] {'mp'}, dimensions={1}, use_global_device_ids=true | all-gather | bytes 884736 | tf_op jit(solution)/shard_map/all_gather | solution.py:161
  293.5 4.1 convolution_convert_fusion
  298.6 4.7 %all-to-all-start.3 = ((bf16[384,8,128]{2,0,1:T(8,128)(2,1)}), bf16[384,8,128]{2,0,1:T(8,128)(2,1)S(1)}, u32[]{:S(2)}, u32[]{:S(2)}) async-start(bf16[384,8,128]{2,0,1:T(8,128)(2,1)} %copy_bitcast_fusion), calls=%async_computation.3 | async-start | bytes 1572864 | tf_op jit(solution)/shard_map/all_to_all | solution.py:41
  303.3 15.4 %all-to-all-done.3 = bf16[384,8,128]{2,0,1:T(8,128)(2,1)S(1)} async-done(((bf16[384,8,128]{2,0,1:T(8,128)(2,1)}), bf16[384,8,128]{2,0,1:T(8,128)(2,1)S(1)}, u32[]{:S(2)}, u32[]{:S(2)}) %all-to-all-start.3) | async-done | bytes 786464 | tf_op jit(solution)/shard_map/all_to_all | solution.py:41
  318.9 1.4 gather_fusion.3
  320.3 2.5 gather_fusion.4
  322.9 8.9 %all-to-all-start.4 = ((bf16[32,24,128]{2,1,0:T(8,128)(2,1)}), bf16[32,24,128]{2,1,0:T(8,128)(2,1)S(1)}, u32[]{:S(2)}, u32[]{:S(2)}) async-start(bf16[32,24,128]{2,1,0:T(8,128)(2,1)} %bitcast.12), calls=%async_computation.4 | async-start | bytes 393216 | tf_op jit(solution)/shard_map/all_to_all | solution.py:176
  332.7 8.5 %all-to-all-done.4 = bf16[32,24,128]{2,1,0:T(8,128)(2,1)S(1)} async-done(((bf16[32,24,128]{2,1,0:T(8,128)(2,1)}), bf16[32,24,128]{2,1,0:T(8,128)(2,1)S(1)}, u32[]{:S(2)}, u32[]{:S(2)}) %all-to-all-start.4) | async-done | bytes 196640 | tf_op jit(solution)/shard_map/all_to_all | solution.py:176
  341.2 2.9 gather_fusion.5
  345.1 6.3 %all-to-all-start.5 = ((bf16[8,144,128]{2,1,0:T(8,128)(2,1)}), bf16[8,144,128]{2,1,0:T(8,128)(2,1)S(1)}, u32[]{:S(2)}, u32[]{:S(2)}) async-start(bf16[8,144,128]{2,1,0:T(8,128)(2,1)} %broadcast_select_fusion.1), calls=%async_computation.5 | async-start | bytes 589824 | tf_op jit(solution)/shard_map/all_to_all | solution.py:184
  352.9 5.2 %all-to-all-done.5 = bf16[8,144,128]{2,1,0:T(8,128)(2,1)S(1)} async-done(((bf16[8,144,128]{2,1,0:T(8,128)(2,1)}), bf16[8,144,128]{2,1,0:T(8,128)(2,1)S(1)}, u32[]{:S(2)}, u32[]{:S(2)}) %all-to-all-start.5) | async-done | bytes 294944 | tf_op jit(solution)/shard_map/all_to_all | solution.py:184
  358.1 5.0 %all-to-all-start.6 = ((bf16[128,8,144]{0,2,1:T(8,128)(2,1)}), bf16[128,8,144]{0,2,1:T(8,128)(2,1)}, u32[]{:S(2)}, u32[]{:S(2)}) async-start(bf16[128,8,144]{0,2,1:T(8,128)(2,1)} %bitcast.85), calls=%async_computation.6 | async-start | bytes 589824 | tf_op jit(solution)/shard_map/all_to_all | solution.py:233
  363.2 2.1 fusion.25
  365.3 3.5 collective-permute-start
  368.9 10.7 %collective-permute-start.1 = (bf16[768,12]{0,1:T(8,128)(2,1)S(1)}, bf16[768,12]{0,1:T(8,128)(2,1)S(1)}, u32[]{:S(2)}, u32[]{:S(2)}) collective-permute-start(bf16[768,12]{0,1:T(8,128)(2,1)S(1)} %get-tuple-element.162), channel_id=1, source_target_pairs={{1,0},{2,1},{3,2},{4,3},{5,4},{6,5},{7,6},{8,7},{9,8},{10,9},{11,1... | collective-permute-start | bytes 55304 | tf_op jit(solution)/shard_map/ppermute | solution.py:201
  413.0 1.5 fusion.82
  426.1 2.3 convert_bitcast_fusion
  430.2 12.0 %all_to_all.68 = bf16[8,128,144]{1,2,0:T(8,128)(2,1)S(1)} all-to-all(bf16[8,128,144]{1,2,0:T(8,128)(2,1)S(1)} %copy.206), channel_id=1, replica_groups=mesh['seq'=32,'mp'=8] {'mp'}, dimensions={0} | all-to-all | bytes 589824 | tf_op jit(solution)/shard_map/all_to_all | solution.py:239
  (311 shorter events, 106.1 us)
Async XLA Ops:
  7.2 286.3 %copy-start = (bf16[512,1024]{1,0:T(8,128)(2,1)S(1)}, bf16[512,1024]{1,0:T(8,128)(2,1)}, u32[]{:S(2)}) copy-start(bf16[512,1024]{1,0:T(8,128)(2,1)} %param.22) | copy-start | bytes 3145732
  9.9 20.5 %all-to-all-start = ((s32[32,1,1]{2,1,0:T(1,128)}), s32[32,1,1]{2,1,0:T(1,128)S(1)}, u32[]{:S(2)}, u32[]{:S(2)}) async-start(s32[32,1,1]{2,1,0:T(1,128)} %broadcast_in_dim.95), calls=%async_computation | async-start | bytes 32768 | tf_op jit(solution)/shard_map/all_to_all | solution.py:34
  42.5 4.7 %copy-start.2 = (bf16[1152,128]{1,0:T(8,128)(2,1)S(1)}, bf16[1152,128]{1,0:T(8,128)(2,1)}, u32[]{:S(2)}) copy-start(bf16[1152,128]{1,0:T(8,128)(2,1)} %param.15) | copy-start | bytes 884740
  47.0 9.3 %copy-start.5 = (bf16[1024,3,128]{2,0,1:T(8,128)(2,1)S(1)}, bf16[1024,3,128]{2,0,1:T(8,128)(2,1)}, u32[]{:S(2)}) copy-start(bf16[1024,3,128]{2,0,1:T(8,128)(2,1)} %param.19) | copy-start | bytes 2359300
  49.9 15.7 %all-to-all-start.1 = ((bf16[32,24,128]{2,1,0:T(8,128)(2,1)}), bf16[32,24,128]{2,1,0:T(8,128)(2,1)S(1)}, u32[]{:S(2)}, u32[]{:S(2)}) async-start(bf16[32,24,128]{2,1,0:T(8,128)(2,1)} %broadcast_select_fusion.2), calls=%async_computation.1 | async-start | bytes 393216 | tf_op jit(solution)/shard_map/all_to_all | solution.py:95
  56.2 117.2 %all-gather.6.cloned.1.call-start = ((), (), s32[]{:S(2)}) async-start(), calls=%async_computation.8 | async-start | bytes 6488064 | tf_op jit(solution)/shard_map/all_gather | solution.py:124
  57.5 31.5 %copy-start.6 = (bf16[1024,3,128]{0,2,1:T(8,128)(2,1)S(1)}, bf16[1024,3,128]{0,2,1:T(8,128)(2,1)}, u32[]{:S(2)}) copy-start(bf16[1024,3,128]{0,2,1:T(8,128)(2,1)} %copy.164) | copy-start | bytes 2359300
  89.7 86.9 %copy-start.4 = (bf16[384,384]{0,1:T(8,128)(2,1)}, bf16[384,384]{0,1:T(8,128)(2,1)S(1)}, u32[]{:S(2)}) copy-start(bf16[384,384]{0,1:T(8,128)(2,1)S(1)} %convolution_convert_fusion.2) | copy-start | bytes 884740
  90.5 272.7 %all-gather.8.cloned.1.call-start = ((), (), s32[]{:S(2)}) async-start(), calls=%async_computation.9 | async-start | bytes 1769472 | tf_op jit(solution)/shard_map/all_gather | solution.py:187
  181.9 2.8 slice-start
  184.6 70.6 %copy-start.9 = (bf16[128,1024]{1,0:T(8,128)(2,1)S(1)}, bf16[128,1024]{1,0:T(8,128)(2,1)}, u32[]{:S(2)}) copy-start(bf16[128,1024]{1,0:T(8,128)(2,1)} %param.20) | copy-start | bytes 786436
  255.2 9.0 %copy-start.7 = (bf16[4,7,96,48]{2,3,1,0:T(8,128)(2,1)S(1)}, bf16[4,7,96,48]{2,3,1,0:T(8,128)(2,1)}, u32[]{:S(2)}) copy-start(bf16[4,7,96,48]{2,3,1,0:T(8,128)(2,1)} %param.25) | copy-start | bytes 774148
  256.7 19.7 %all-to-all-start.2 = ((bf16[384,8,128]{2,0,1:T(8,128)(2,1)}), bf16[384,8,128]{2,0,1:T(8,128)(2,1)S(1)}, u32[]{:S(2)}, u32[]{:S(2)}) async-start(bf16[384,8,128]{2,0,1:T(8,128)(2,1)} %copy_bitcast_fusion.1), calls=%async_computation.2 | async-start | bytes 1572864 | tf_op jit(solution)/shard_map/all_to_all | solution.py:41
  264.2 117.3 %all-gather.10.cloned.1.call-start = ((), (), s32[]{:S(2)}) async-start(), calls=%async_computation.10 | async-start | bytes 6193152 | tf_op jit(solution)/shard_map/all_gather | solution.py:188
  298.6 33.1 %copy-start.10 = (s32[1152]{0:T(1024)S(1)}, s32[1152]{0:T(1024)}, u32[]{:S(2)}) copy-start(s32[1152]{0:T(1024)} %param.16) | copy-start | bytes 13828
  298.6 20.1 %all-to-all-start.3 = ((bf16[384,8,128]{2,0,1:T(8,128)(2,1)}), bf16[384,8,128]{2,0,1:T(8,128)(2,1)S(1)}, u32[]{:S(2)}, u32[]{:S(2)}) async-start(bf16[384,8,128]{2,0,1:T(8,128)(2,1)} %copy_bitcast_fusion), calls=%async_computation.3 | async-start | bytes 1572864 | tf_op jit(solution)/shard_map/all_to_all | solution.py:41
  318.9 26.2 %copy-start.3 = (bf16[384,128]{1,0:T(8,128)(2,1)}, bf16[384,128]{1,0:T(8,128)(2,1)S(1)}, u32[]{:S(2)}) copy-start(bf16[384,128]{1,0:T(8,128)(2,1)S(1)} %add_convert_fusion) | copy-start | bytes 294916
  320.3 31.6 %copy-start.8 = (bf16[128,1152]{1,0:T(8,128)(2,1)S(1)}, bf16[128,1152]{1,0:T(8,128)(2,1)}, u32[]{:S(2)}) copy-start(bf16[128,1152]{1,0:T(8,128)(2,1)} %param.27) | copy-start | bytes 884740
  322.9 18.3 %all-to-all-start.4 = ((bf16[32,24,128]{2,1,0:T(8,128)(2,1)}), bf16[32,24,128]{2,1,0:T(8,128)(2,1)S(1)}, u32[]{:S(2)}, u32[]{:S(2)}) async-start(bf16[32,24,128]{2,1,0:T(8,128)(2,1)} %bitcast.12), calls=%async_computation.4 | async-start | bytes 393216 | tf_op jit(solution)/shard_map/all_to_all | solution.py:176
  345.1 13.0 %all-to-all-start.5 = ((bf16[8,144,128]{2,1,0:T(8,128)(2,1)}), bf16[8,144,128]{2,1,0:T(8,128)(2,1)S(1)}, u32[]{:S(2)}, u32[]{:S(2)}) async-start(bf16[8,144,128]{2,1,0:T(8,128)(2,1)} %broadcast_select_fusion.1), calls=%async_computation.5 | async-start | bytes 589824 | tf_op jit(solution)/shard_map/all_to_all | solution.py:184
  351.3 74.7 %all-gather.12.cloned.1.call-start = ((), (), s32[]{:S(2)}) async-start(), calls=%async_computation.11 | async-start | bytes 1769472 | tf_op jit(solution)/shard_map/all_gather | solution.py:191
  358.1 70.8 %all-to-all-start.6 = ((bf16[128,8,144]{0,2,1:T(8,128)(2,1)}), bf16[128,8,144]{0,2,1:T(8,128)(2,1)}, u32[]{:S(2)}, u32[]{:S(2)}) async-start(bf16[128,8,144]{0,2,1:T(8,128)(2,1)} %bitcast.85), calls=%async_computation.6 | async-start | bytes 589824 | tf_op jit(solution)/shard_map/all_to_all | solution.py:233
  365.3 14.5 %collective-permute-start = (bf16[768,12]{0,1:T(8,128)(2,1)S(1)}, bf16[768,12]{0,1:T(8,128)(2,1)S(1)}, u32[]{:S(2)}, u32[]{:S(2)}) collective-permute-start(bf16[768,12]{0,1:T(8,128)(2,1)S(1)} %get-tuple-element.161), channel_id=1, source_target_pairs={{0,1},{1,2},{2,3},{3,4},{4,5},{5,6},{6,7},{7,8},{8,9},{9,10},{10,1... | collective-permute-start | bytes 55304 | tf_op jit(solution)/shard_map/ppermute | solution.py:200
  368.9 11.0 %collective-permute-start.1 = (bf16[768,12]{0,1:T(8,128)(2,1)S(1)}, bf16[768,12]{0,1:T(8,128)(2,1)S(1)}, u32[]{:S(2)}, u32[]{:S(2)}) collective-permute-start(bf16[768,12]{0,1:T(8,128)(2,1)S(1)} %get-tuple-element.162), channel_id=1, source_target_pairs={{1,0},{2,1},{3,2},{4,3},{5,4},{6,5},{7,6},{8,7},{9,8},{10,9},{11,1... | collective-permute-start | bytes 55304 | tf_op jit(solution)/shard_map/ppermute | solution.py:201
  426.1 17.0 %copy-start.1 = (bf16[512,1024]{1,0:T(8,128)(2,1)S(1)}, bf16[512,1024]{1,0:T(8,128)(2,1)}, u32[]{:S(2)}) copy-start(bf16[512,1024]{1,0:T(8,128)(2,1)} %param.22) | copy-start | bytes 3145732
Sparse Core Ops, SparseCore 0:
  90.6 82.6 all-gather.5
  175.2 31.6 all-gather.7
  266.8 48.2 all-gather.9
  353.6 23.2 all-gather.11
where the time goes:
time: 458 us; the launch traced here: 450 us
  waiting for transfers between devices  134 us (29%)
  matrix products  105 us (23%)
  starting transfers between devices  65 us (14%)
  local copies, waits for them, and re-layouts  58.4 us (13%)
  blocking collectives  45.6 us (10%)
  other arithmetic  25.3 us (6%)
  between operations  14.9 us (3%)
    all_gather x1, waiting for transfers between devices, local(): lax.all_gather(projected[:, feature_width:], 'seq', axis=0, tiled=True)  82.1 us
    dot_general x28, matrix products, local(): jnp.einsum('goi,gif->gof', kernel[tap_index], tap, preferred_element_type...  32.7 us
    dot_general x24, matrix products, advance(): jnp.einsum('qhd,khd->hqk', queries, block_keys, preferred_element_type=jn...  32 us
    dot_general x24, matrix products, advance(): jnp.einsum('hqk,khd->qhd', expo.astype(jnp.bfloat16), block_values, prefe...  31 us
    all_to_all x2, waiting for transfers between devices, sum_scatter(): moved = lax.all_to_all(split, axis, dim, dim, tiled=True)  26.4 us
    all_gather x1, blocking collectives, local(): gathered = lax.all_gather(packed, 'mp', axis=1, tiled=True)  17.1 us
    all_gather x1, blocking collectives, local(): gathered_two = lax.all_gather(first_out, 'mp', axis=1, tiled=True)  16.4 us
    unnamed x31, local copies, waits for them, and re-layouts  12.2 us
  transfers between devices with their start and end apart: 13, of which 7 were waited for; matrix products, arithmetic and copies ran while one was open for 35% of the time, Pallas kernels for 0%

commit v1 on v0

--- a/solution.py
+++ b/solution.py
@@ -122,16 +122,14 @@
     )
     carry = start_state
     key_value = lax.all_gather(projected[:, feature_width:], "seq", axis=0, tiled=True)
-    piece_keys = key_value[:, :feature_width]
-    piece_values = key_value[:, feature_width:]
-    piece_rows = piece_keys.shape[0]
+    piece_rows = key_value.shape[0]
     block_rows = math.gcd(piece_rows, 512)
-    piece_keys = piece_keys.reshape(piece_rows // block_rows, block_rows, heads_local, HEAD_DIM)
-    piece_values = piece_values.reshape(piece_rows // block_rows, block_rows, heads_local, HEAD_DIM)
+    piece_pairs = key_value.reshape(piece_rows // block_rows, block_rows, 2, heads_local, HEAD_DIM)
 
     def advance(state, block_pair):
         running_max, totals, weighted = state
-        block_keys, block_values = block_pair
+        block_keys = block_pair[:, 0]
+        block_values = block_pair[:, 1]
         scores = (
             jnp.einsum("qhd,khd->hqk", queries, block_keys, preferred_element_type=jnp.float32)
             * score_scale
@@ -148,7 +146,7 @@
         )
         return ((new_max, totals, weighted), None)
 
-    carry, _ = lax.scan(advance, carry, (piece_keys, piece_values))
+    carry, _ = lax.scan(advance, carry, piece_pairs)
     running_max, totals, weighted = carry
     attended = (
         (weighted / jnp.transpose(totals)[:, :, None])

time: 458 us -> 439 us (0.959)
  matrix products: 105 us -> 63.7 us
  local copies, waits for them, and re-layouts: 58.4 us -> 82 us
    squeeze x0 -> x24, local copies, waits for them, and re-layouts: none -> 23.3 us  [local(): carry, _ = lax.scan(advance, carry, piece_pairs)]
    dot_general x24, matrix products: 31 us -> 9.15 us  [advance(): jnp.einsum('hqk,khd->qhd', expo.astype(jnp.bfloat16), block_values, prefe...]
    dot_general x24, matrix products: 32 us -> 10.3 us  [advance(): jnp.einsum('qhd,khd->hqk', queries, block_keys, preferred_element_type=jn...]
    unnamed x31 -> x23, local copies, waits for them, and re-layouts: 12.2 us -> 15.7 us
  transfers between devices with their start and end apart: 13 -> 13, of which waited for: 7 -> 7; matrix products, arithmetic and copies ran while one was open for 35% -> 32% of each run, Pallas kernels for 0% -> 0%
where the time goes in v1:
time: 439 us; the launch traced here: 431 us
  waiting for transfers between devices  133 us (30%)
  local copies, waits for them, and re-layouts  82 us (19%)
  starting transfers between devices  64.9 us (15%)
  matrix products  63.7 us (15%)
  blocking collectives  45.6 us (10%)
  other arithmetic  25.3 us (6%)
  between operations  14.9 us (3%)
    all_gather x1, waiting for transfers between devices, local(): lax.all_gather(projected[:, feature_width:], 'seq', axis=0, tiled=True)  82.1 us
    dot_general x28, matrix products, local(): jnp.einsum('goi,gif->gof', kernel[tap_index], tap, preferred_element_type...  32.7 us
    all_to_all x2, waiting for transfers between devices, sum_scatter(): moved = lax.all_to_all(split, axis, dim, dim, tiled=True)  25.5 us
    squeeze x24, local copies, waits for them, and re-layouts, local(): carry, _ = lax.scan(advance, carry, piece_pairs)  23.3 us
    all_gather x1, blocking collectives, local(): gathered = lax.all_gather(packed, 'mp', axis=1, tiled=True)  17.1 us
    all_gather x1, blocking collectives, local(): gathered_two = lax.all_gather(first_out, 'mp', axis=1, tiled=True)  16.5 us
    unnamed x23, local copies, waits for them, and re-layouts  15.7 us
    all_to_all x2, starting transfers between devices, sum_scatter(): moved = lax.all_to_all(split, axis, dim, dim, tiled=True)  12.1 us
  transfers between devices with their start and end apart: 13, of which 7 were waited for; matrix products, arithmetic and copies ran while one was open for 32% of the time, Pallas kernels for 0%

profile of v1, /device:TPU:1, one launch (start us, length us, event | category | flops | bytes accessed | tf_op | source)
XLA Modules:
  0.0 431.0 jit_solution(7312773838394476862)
XLA Ops:
  7.2 1.4 reduce_sum.155
  8.6 1.3 broadcast_in_dim.95
  9.9 11.9 %all-to-all-start = ((s32[32,1,1]{2,1,0:T(1,128)}), s32[32,1,1]{2,1,0:T(1,128)S(1)}, u32[]{:S(2)}, u32[]{:S(2)}) async-start(s32[32,1,1]{2,1,0:T(1,128)} %broadcast_in_dim.95), calls=%async_computation | async-start | bytes 32768 | tf_op jit(solution)/shard_map/all_to_all | solution.py:34
  23.6 2.9 scatter_custom_fusion.2
  27.3 3.0 all-to-all-done
  33.1 1.4 subtract_compare_fusion
  34.6 1.4 compare_select_fusion.2
  36.1 6.4 %scatter_custom_fusion = s32[1152]{0:T(1024)S(1)} fusion(s32[1152]{0:T(1024)S(1)} %get-tuple-element.147, s32[1152]{0:T(1024)S(1)} %iota.25, s32[]{:T(128)} %constant.70.clone.1), kind=kCustom, calls=%fused_computation.313 | custom fusion | bytes 4612 | tf_op jit(solution)/shard_map/scatter | solution.py:86
  42.5 4.5 %gather_fusion = s32[768]{0:T(1024)S(1)} fusion(s32[1152]{0:T(1024)S(1)} %scatter_custom_fusion, s32[1024]{0:T(1024)S(1)} %pad_clamp_fusion.5), kind=kCustom, calls=%fused_computation | custom fusion | bytes 9216 | tf_op jit(solution)/shard_map/gather | solution.py:93
  47.2 1.9 gather_fusion.1
  49.9 6.3 %all-to-all-start.1 = ((bf16[32,24,128]{2,1,0:T(8,128)(2,1)}), bf16[32,24,128]{2,1,0:T(8,128)(2,1)S(1)}, u32[]{:S(2)}, u32[]{:S(2)}) async-start(bf16[32,24,128]{2,1,0:T(8,128)(2,1)} %broadcast_select_fusion.2), calls=%async_computation.1 | async-start | bytes 393216 | tf_op jit(solution)/shard_map/all_to_all | solution.py:95
  57.8 7.8 %all-to-all-done.1 = bf16[32,24,128]{2,1,0:T(8,128)(2,1)S(1)} async-done(((bf16[32,24,128]{2,1,0:T(8,128)(2,1)}), bf16[32,24,128]{2,1,0:T(8,128)(2,1)S(1)}, u32[]{:S(2)}, u32[]{:S(2)}) %all-to-all-start.1) | async-done | bytes 196640 | tf_op jit(solution)/shard_map/all_to_all | solution.py:95
  65.6 4.2 scatter_custom_fusion.1
  69.9 1.4 gather_fusion.2
  71.3 17.1 %all-gather = bf16[384,1024]{1,0:T(8,128)(2,1)S(1)} all-gather(bf16[384,128]{1,0:T(8,128)(2,1)S(1)} %gather_fusion.2), channel_id=2, replica_groups=mesh['seq'=32,'mp'=8] {'mp'}, dimensions={1}, use_global_device_ids=true | all-gather | bytes 884736 | tf_op jit(solution)/shard_map/all_gather | solution.py:111
  89.0 1.9 convolution_convert_fusion.2
  92.4 82.1 %all-gather.6.cloned.1.call-done = bf16[12288,256]{0,1:T(8,128)(2,1)} async-done(((bf16[384,256]{0,1:T(8,128)(2,1)}), bf16[12288,256]{0,1:T(8,128)(2,1)}) %all-gather.6.cloned.1.call-update) | async-done | bytes 6291472 | tf_op jit(solution)/shard_map/all_gather | solution.py:124
  174.5 5.6 %copy.206 = bf16[32,8,24,512]{3,2,1,0:T(8,128)(2,1)S(1)} copy(bf16[32,8,24,512]{3,1,2,0:T(8,128)(2,1)} %bitcast.307) | data formatting | bytes 12582912
  180.1 4.9 %copy.161 = bf16[24,512,2,2,64]{1,4,3,2,0:T(8,128)(2,1)} copy(bf16[24,512,2,2,64]{1,0,4,3,2:T(8,128)(2,1)S(1)} %bitcast.302) | data formatting | bytes 12582912
  185.0 50.3 %while.15 = (s32[]{:T(128)}, f32[2,384]{1,0:T(2,128)S(1)}, f32[2,384]{1,0:T(2,128)S(1)}, f32[384,2,64]{0,2,1:T(8,128)S(1)}, bf16[24,512,2,2,64]{1,4,3,2,0:T(8,12...) while((s32[]{:T(128)}, f32[2,384]{1,0:T(2,128)S(1)}, ...), condition=%wide.region_12.13_spmd.clone, body=%wide.region_9.12_spmd.clone.sunk | while | flops 103174656 | bytes 6045797 | solution.py:149
  235.4 1.3 convolution_convert_fusion.1
  237.8 7.6 %all-to-all-start.2 = ((bf16[384,8,128]{2,0,1:T(8,128)(2,1)}), bf16[384,8,128]{2,0,1:T(8,128)(2,1)S(1)}, u32[]{:S(2)}, u32[]{:S(2)}) async-start(bf16[384,8,128]{2,0,1:T(8,128)(2,1)} %copy_bitcast_fusion.1), calls=%async_computation.2 | async-start | bytes 1572864 | tf_op jit(solution)/shard_map/all_to_all | solution.py:41
  245.4 2.1 copy.166
  247.5 10.0 %all-to-all-done.2 = bf16[384,8,128]{2,0,1:T(8,128)(2,1)S(1)} async-done(((bf16[384,8,128]{2,0,1:T(8,128)(2,1)}), bf16[384,8,128]{2,0,1:T(8,128)(2,1)S(1)}, u32[]{:S(2)}, u32[]{:S(2)}) %all-to-all-start.2) | async-done | bytes 786464 | tf_op jit(solution)/shard_map/all_to_all | solution.py:41
  257.7 16.5 %all_gather.20 = bf16[384,1024]{1,0:T(8,128)(2,1)S(1)} all-gather(bf16[384,128]{1,0:T(8,128)(2,1)S(1)} %add_convert_fusion.1), channel_id=1, replica_groups=mesh['seq'=32,'mp'=8] {'mp'}, dimensions={1}, use_global_device_ids=true | all-gather | bytes 884736 | tf_op jit(solution)/shard_map/all_gather | solution.py:159
  274.7 4.0 convolution_convert_fusion
  279.9 4.5 %all-to-all-start.3 = ((bf16[384,8,128]{2,0,1:T(8,128)(2,1)}), bf16[384,8,128]{2,0,1:T(8,128)(2,1)S(1)}, u32[]{:S(2)}, u32[]{:S(2)}) async-start(bf16[384,8,128]{2,0,1:T(8,128)(2,1)} %copy_bitcast_fusion), calls=%async_computation.3 | async-start | bytes 1572864 | tf_op jit(solution)/shard_map/all_to_all | solution.py:41
  284.4 15.5 %all-to-all-done.3 = bf16[384,8,128]{2,0,1:T(8,128)(2,1)S(1)} async-done(((bf16[384,8,128]{2,0,1:T(8,128)(2,1)}), bf16[384,8,128]{2,0,1:T(8,128)(2,1)S(1)}, u32[]{:S(2)}, u32[]{:S(2)}) %all-to-all-start.3) | async-done | bytes 786464 | tf_op jit(solution)/shard_map/all_to_all | solution.py:41
  300.0 1.4 gather_fusion.3
  301.5 2.5 gather_fusion.4
  304.0 8.9 %all-to-all-start.4 = ((bf16[32,24,128]{2,1,0:T(8,128)(2,1)}), bf16[32,24,128]{2,1,0:T(8,128)(2,1)S(1)}, u32[]{:S(2)}, u32[]{:S(2)}) async-start(bf16[32,24,128]{2,1,0:T(8,128)(2,1)} %bitcast.12), calls=%async_computation.4 | async-start | bytes 393216 | tf_op jit(solution)/shard_map/all_to_all | solution.py:174
  313.8 8.5 %all-to-all-done.4 = bf16[32,24,128]{2,1,0:T(8,128)(2,1)S(1)} async-done(((bf16[32,24,128]{2,1,0:T(8,128)(2,1)}), bf16[32,24,128]{2,1,0:T(8,128)(2,1)S(1)}, u32[]{:S(2)}, u32[]{:S(2)}) %all-to-all-start.4) | async-done | bytes 196640 | tf_op jit(solution)/shard_map/all_to_all | solution.py:174
  322.3 2.9 gather_fusion.5
  326.2 6.2 %all-to-all-start.5 = ((bf16[8,144,128]{2,1,0:T(8,128)(2,1)}), bf16[8,144,128]{2,1,0:T(8,128)(2,1)S(1)}, u32[]{:S(2)}, u32[]{:S(2)}) async-start(bf16[8,144,128]{2,1,0:T(8,128)(2,1)} %broadcast_select_fusion.1), calls=%async_computation.5 | async-start | bytes 589824 | tf_op jit(solution)/shard_map/all_to_all | solution.py:182
  334.0 5.2 %all-to-all-done.5 = bf16[8,144,128]{2,1,0:T(8,128)(2,1)S(1)} async-done(((bf16[8,144,128]{2,1,0:T(8,128)(2,1)}), bf16[8,144,128]{2,1,0:T(8,128)(2,1)S(1)}, u32[]{:S(2)}, u32[]{:S(2)}) %all-to-all-start.5) | async-done | bytes 294944 | tf_op jit(solution)/shard_map/all_to_all | solution.py:182
  339.2 5.0 %all-to-all-start.6 = ((bf16[128,8,144]{0,2,1:T(8,128)(2,1)}), bf16[128,8,144]{0,2,1:T(8,128)(2,1)}, u32[]{:S(2)}, u32[]{:S(2)}) async-start(bf16[128,8,144]{0,2,1:T(8,128)(2,1)} %bitcast.85), calls=%async_computation.6 | async-start | bytes 589824 | tf_op jit(solution)/shard_map/all_to_all | solution.py:231
  344.4 2.1 fusion.19
  346.5 3.5 collective-permute-start
  350.0 10.7 %collective-permute-start.1 = (bf16[768,12]{0,1:T(8,128)(2,1)S(1)}, bf16[768,12]{0,1:T(8,128)(2,1)S(1)}, u32[]{:S(2)}, u32[]{:S(2)}) collective-permute-start(bf16[768,12]{0,1:T(8,128)(2,1)S(1)} %get-tuple-element.145), channel_id=1, source_target_pairs={{1,0},{2,1},{3,2},{4,3},{5,4},{6,5},{7,6},{8,7},{9,8},{10,9},{11,1... | collective-permute-start | bytes 55304 | tf_op jit(solution)/shard_map/ppermute | solution.py:199
  363.8 1.2 convolution_add_fusion.23
  367.3 1.2 convolution_add_fusion.20
  368.5 1.2 convolution_add_fusion.19
  369.7 1.2 fusion.189
  371.2 1.3 fusion.52
  374.1 1.2 fusion.130
  375.2 1.2 convolution_add_fusion.17
  376.4 1.2 convolution_add_fusion.16
  377.6 1.2 convolution_add_fusion.15
  378.8 1.2 convolution_add_fusion.14
  379.9 1.2 convolution_add_fusion.13
  381.1 1.2 fusion.190
  382.7 1.3 fusion.64
  385.5 1.2 fusion.129
  386.7 1.2 convolution_add_fusion.11
  389.0 1.2 convolution_add_fusion.9
  390.2 1.2 convolution_add_fusion.8
  391.4 1.2 convolution_add_fusion.7
  392.5 1.2 fusion.191
  394.1 1.5 fusion.76
  404.1 1.2 fusion.192
  405.6 1.2 fusion.88
  407.2 2.3 convert_bitcast_fusion
  410.0 1.2 fusion.48
  411.3 12.0 %all_to_all.68 = bf16[8,128,144]{1,2,0:T(8,128)(2,1)S(1)} all-to-all(bf16[8,128,144]{1,2,0:T(8,128)(2,1)S(1)} %copy.201), channel_id=1, replica_groups=mesh['seq'=32,'mp'=8] {'mp'}, dimensions={0} | all-to-all | bytes 589824 | tf_op jit(solution)/shard_map/all_to_all | solution.py:237
  (326 shorter events, 87.0 us)
Async XLA Ops:
  7.2 267.5 %copy-start = (bf16[512,1024]{1,0:T(8,128)(2,1)S(1)}, bf16[512,1024]{1,0:T(8,128)(2,1)}, u32[]{:S(2)}) copy-start(bf16[512,1024]{1,0:T(8,128)(2,1)} %param.22) | copy-start | bytes 3145732
  9.9 20.5 %all-to-all-start = ((s32[32,1,1]{2,1,0:T(1,128)}), s32[32,1,1]{2,1,0:T(1,128)S(1)}, u32[]{:S(2)}, u32[]{:S(2)}) async-start(s32[32,1,1]{2,1,0:T(1,128)} %broadcast_in_dim.95), calls=%async_computation | async-start | bytes 32768 | tf_op jit(solution)/shard_map/all_to_all | solution.py:34
  42.5 4.7 %copy-start.2 = (bf16[1152,128]{1,0:T(8,128)(2,1)S(1)}, bf16[1152,128]{1,0:T(8,128)(2,1)}, u32[]{:S(2)}) copy-start(bf16[1152,128]{1,0:T(8,128)(2,1)} %param.15) | copy-start | bytes 884740
  42.5 13.8 %copy-start.5 = (bf16[1024,3,128]{2,0,1:T(8,128)(2,1)S(1)}, bf16[1024,3,128]{2,0,1:T(8,128)(2,1)}, u32[]{:S(2)}) copy-start(bf16[1024,3,128]{2,0,1:T(8,128)(2,1)} %param.19) | copy-start | bytes 2359300
  49.9 15.7 %all-to-all-start.1 = ((bf16[32,24,128]{2,1,0:T(8,128)(2,1)}), bf16[32,24,128]{2,1,0:T(8,128)(2,1)S(1)}, u32[]{:S(2)}, u32[]{:S(2)}) async-start(bf16[32,24,128]{2,1,0:T(8,128)(2,1)} %broadcast_select_fusion.2), calls=%async_computation.1 | async-start | bytes 393216 | tf_op jit(solution)/shard_map/all_to_all | solution.py:95
  56.2 118.3 %all-gather.6.cloned.1.call-start = ((), (), s32[]{:S(2)}) async-start(), calls=%async_computation.8 | async-start | bytes 6488064 | tf_op jit(solution)/shard_map/all_gather | solution.py:124
  90.8 89.3 %copy-start.4 = (bf16[384,384]{0,1:T(8,128)(2,1)}, bf16[384,384]{0,1:T(8,128)(2,1)S(1)}, u32[]{:S(2)}) copy-start(bf16[384,384]{0,1:T(8,128)(2,1)S(1)} %convolution_convert_fusion.2) | copy-start | bytes 884740
  91.6 252.7 %all-gather.8.cloned.1.call-start = ((), (), s32[]{:S(2)}) async-start(), calls=%async_computation.9 | async-start | bytes 1769472 | tf_op jit(solution)/shard_map/all_gather | solution.py:185
  180.1 4.9 %slice-start = ((bf16[384,384]{0,1:T(8,128)(2,1)}), bf16[384,128]{0,1:T(8,128)(2,1)S(1)}, s32[]{:S(2)}) async-start(bf16[384,384]{0,1:T(8,128)(2,1)} %copy-done.4), calls=%async_computation.12 | async-start | bytes 196608 | tf_op jit(solution)/shard_map/slice | solution.py:116
  237.8 19.8 %all-to-all-start.2 = ((bf16[384,8,128]{2,0,1:T(8,128)(2,1)}), bf16[384,8,128]{2,0,1:T(8,128)(2,1)S(1)}, u32[]{:S(2)}, u32[]{:S(2)}) async-start(bf16[384,8,128]{2,0,1:T(8,128)(2,1)} %copy_bitcast_fusion.1), calls=%async_computation.2 | async-start | bytes 1572864 | tf_op jit(solution)/shard_map/all_to_all | solution.py:41
  245.4 117.2 %all-gather.10.cloned.1.call-start = ((), (), s32[]{:S(2)}) async-start(), calls=%async_computation.10 | async-start | bytes 6193152 | tf_op jit(solution)/shard_map/all_gather | solution.py:186
  278.8 34.1 %copy-start.7 = (s32[1152]{0:T(1024)S(1)}, s32[1152]{0:T(1024)}, u32[]{:S(2)}) copy-start(s32[1152]{0:T(1024)} %param.16) | copy-start | bytes 13828
  278.8 54.2 %copy-start.6 = (bf16[128,1152]{1,0:T(8,128)(2,1)S(1)}, bf16[128,1152]{1,0:T(8,128)(2,1)}, u32[]{:S(2)}) copy-start(bf16[128,1152]{1,0:T(8,128)(2,1)} %param.27) | copy-start | bytes 884740
  279.9 20.0 %all-to-all-start.3 = ((bf16[384,8,128]{2,0,1:T(8,128)(2,1)}), bf16[384,8,128]{2,0,1:T(8,128)(2,1)S(1)}, u32[]{:S(2)}, u32[]{:S(2)}) async-start(bf16[384,8,128]{2,0,1:T(8,128)(2,1)} %copy_bitcast_fusion), calls=%async_computation.3 | async-start | bytes 1572864 | tf_op jit(solution)/shard_map/all_to_all | solution.py:41
  300.0 46.4 %copy-start.3 = (bf16[384,128]{1,0:T(8,128)(2,1)}, bf16[384,128]{1,0:T(8,128)(2,1)S(1)}, u32[]{:S(2)}) copy-start(bf16[384,128]{1,0:T(8,128)(2,1)S(1)} %add_convert_fusion) | copy-start | bytes 294916
  304.0 18.3 %all-to-all-start.4 = ((bf16[32,24,128]{2,1,0:T(8,128)(2,1)}), bf16[32,24,128]{2,1,0:T(8,128)(2,1)S(1)}, u32[]{:S(2)}, u32[]{:S(2)}) async-start(bf16[32,24,128]{2,1,0:T(8,128)(2,1)} %bitcast.12), calls=%async_computation.4 | async-start | bytes 393216 | tf_op jit(solution)/shard_map/all_to_all | solution.py:174
  326.2 13.0 %all-to-all-start.5 = ((bf16[8,144,128]{2,1,0:T(8,128)(2,1)}), bf16[8,144,128]{2,1,0:T(8,128)(2,1)S(1)}, u32[]{:S(2)}, u32[]{:S(2)}) async-start(bf16[8,144,128]{2,1,0:T(8,128)(2,1)} %broadcast_select_fusion.1), calls=%async_computation.5 | async-start | bytes 589824 | tf_op jit(solution)/shard_map/all_to_all | solution.py:182
  332.4 74.7 %all-gather.12.cloned.1.call-start = ((), (), s32[]{:S(2)}) async-start(), calls=%async_computation.11 | async-start | bytes 1769472 | tf_op jit(solution)/shard_map/all_gather | solution.py:189
  339.2 70.8 %all-to-all-start.6 = ((bf16[128,8,144]{0,2,1:T(8,128)(2,1)}), bf16[128,8,144]{0,2,1:T(8,128)(2,1)}, u32[]{:S(2)}, u32[]{:S(2)}) async-start(bf16[128,8,144]{0,2,1:T(8,128)(2,1)} %bitcast.85), calls=%async_computation.6 | async-start | bytes 589824 | tf_op jit(solution)/shard_map/all_to_all | solution.py:231
  346.5 14.5 %collective-permute-start = (bf16[768,12]{0,1:T(8,128)(2,1)S(1)}, bf16[768,12]{0,1:T(8,128)(2,1)S(1)}, u32[]{:S(2)}, u32[]{:S(2)}) collective-permute-start(bf16[768,12]{0,1:T(8,128)(2,1)S(1)} %get-tuple-element.144), channel_id=1, source_target_pairs={{0,1},{1,2},{2,3},{3,4},{4,5},{5,6},{6,7},{7,8},{8,9},{9,10},{10,1... | collective-permute-start | bytes 55304 | tf_op jit(solution)/shard_map/ppermute | solution.py:198
  350.0 11.0 %collective-permute-start.1 = (bf16[768,12]{0,1:T(8,128)(2,1)S(1)}, bf16[768,12]{0,1:T(8,128)(2,1)S(1)}, u32[]{:S(2)}, u32[]{:S(2)}) collective-permute-start(bf16[768,12]{0,1:T(8,128)(2,1)S(1)} %get-tuple-element.145), channel_id=1, source_target_pairs={{1,0},{2,1},{3,2},{4,3},{5,4},{6,5},{7,6},{8,7},{9,8},{10,9},{11,1... | collective-permute-start | bytes 55304 | tf_op jit(solution)/shard_map/ppermute | solution.py:199
  407.2 17.0 %copy-start.1 = (bf16[512,1024]{1,0:T(8,128)(2,1)S(1)}, bf16[512,1024]{1,0:T(8,128)(2,1)}, u32[]{:S(2)}) copy-start(bf16[512,1024]{1,0:T(8,128)(2,1)} %param.22) | copy-start | bytes 3145732
Sparse Core Ops, SparseCore 0:
  91.8 82.6 all-gather.5
  176.3 31.6 all-gather.7
  248.0 48.3 all-gather.9
  334.8 23.2 all-gather.11
